TPU v7x, 256 devices: a whole 4x4x8 slice. The times are simulated.
256 devices in a mesh: sector: 64 (over z, y, core), dof: 4 (over x).
Axes of the slice: x: 4, y: 4, z: 8, core: 2. Of those that a mesh axis runs over, the one named last changes fastest.
Arguments:
- load_history: bfloat16 [64, 64, 6144], P('sector', None, 'dof'), may hold values from -6 to 6
- sector_basis: bfloat16 [6144, 1536], P('dof'), may hold values from -0.078125 to 0.078125
- harmonic_modes: bfloat16 [64, 1536, 256], P('sector'), may hold values from -0.15625 to 0.15625
- stress_basis: bfloat16 [1536, 6144], P(None, 'dof'), may hold values from -0.375 to 0.375
- mode_decay: float32 [64, 256], P('sector'), may hold values from 0.01 to 0.3
- mode_phase: float32 [64, 256], P('sector'), may hold values from 0.05 to 1.5
- mode_count: int32 [64], P('sector'), may hold values from 64 to 256, as said below
- slot_harmonic: int32 [64], replicated, may hold values from 0 to 63, each once
Outputs:
- stress_field: bfloat16 [64, 64, 6144], P('sector', None, 'dof')
Inputs may be any that keep to these rules, and one draw needn't show every extreme that they name: Slot modes from mode_count on are left out; some slot has 256 live modes and some 256 // 4. `slot_harmonic`: every harmonic component is held by exactly one slot.
All inputs are finite; a program needn't handle non-finite values.
Results may differ from a plain program's by a relative error of at most 0.025.
Values may be sent and summed in bfloat16 or wider, within the bound.
No kernel may reach another device: no remote copies, remote signals or barrier semaphores. Data moves between devices by JAX's collectives and lax.ppermute only.
A program may use at most 64 MiB of HBM per device.

v0:
```python
import math
import jax
import jax.numpy as jnp
from jax import lax
from jax.sharding import PartitionSpec as P


def transform_table(slot_harmonic):
    count_all = slot_harmonic.shape[0]
    half_count = count_all // 2
    sine_rows = slot_harmonic > half_count
    harmonic_order = jnp.where(sine_rows, slot_harmonic - half_count, slot_harmonic)
    sector_index = jnp.arange(count_all, dtype=jnp.int32)
    residue = harmonic_order[:, None] * sector_index[None, :] % count_all
    phase_angle = residue.astype(jnp.float32) * jnp.float32(2.0 * math.pi / count_all)
    wave_table = jnp.where(sine_rows[:, None], jnp.sin(phase_angle), jnp.cos(phase_angle))
    single = (slot_harmonic == 0) | (slot_harmonic == half_count)
    weight = jnp.where(single, jnp.float32(1.0 / count_all), jnp.float32(2.0 / count_all))
    return jnp.sqrt(weight)[:, None] * wave_table


def filter_kernel(decay_rates, phase_steps, steps_count):
    time_index = jnp.arange(steps_count, dtype=jnp.int32)
    offset = time_index[:, None] - time_index[None, :]
    causal = offset >= 0
    lag_value = jnp.maximum(offset, 0).astype(jnp.float32)
    gain_factor = jnp.sqrt(1.0 - jnp.exp(-2.0 * decay_rates))
    shape_table = (
        gain_factor[..., None, None]
        * jnp.exp(-decay_rates[..., None, None] * lag_value)
        * jnp.cos(phase_steps[..., None, None] * lag_value)
    )
    return jnp.where(causal, shape_table, jnp.float32(0.0))


def local(
    load_history,
    sector_basis,
    harmonic_modes,
    stress_basis,
    mode_decay,
    mode_phase,
    mode_count,
    slot_harmonic,
):
    highest = lax.Precision.HIGHEST
    table = transform_table(slot_harmonic)
    steps_count = load_history.shape[1]
    modes_slot = harmonic_modes[0]
    partial_value = jnp.dot(load_history[0], sector_basis, preferred_element_type=jnp.float32)
    live = (jnp.arange(modes_slot.shape[1], dtype=jnp.int32) < mode_count[0]).astype(jnp.float32)
    kernel = filter_kernel(mode_decay[0], mode_phase[0], steps_count)
    reduced = lax.psum(partial_value.astype(jnp.bfloat16), "dof")
    mixed = jnp.einsum(
        "ks,stc->ktc",
        table,
        lax.all_to_all(reduced[None], "sector", split_axis=1, concat_axis=0, tiled=True).astype(
            jnp.float32
        ),
        precision=highest,
    )
    spectrum = lax.all_to_all(
        mixed.astype(jnp.bfloat16), "sector", split_axis=0, concat_axis=1, tiled=True
    )[0]
    modal = jnp.dot(spectrum, modes_slot, preferred_element_type=jnp.float32) * live[None, :]
    response = jnp.einsum("mtu,um->tm", kernel, modal, precision=highest)
    project_response = response.astype(jnp.bfloat16)
    product = lax.dot_general(
        project_response, modes_slot, (((1,), (1,)), ((), ())), preferred_element_type=jnp.float32
    )
    returned = product.astype(jnp.bfloat16)
    mixed = jnp.einsum(
        "ks,ktc->stc",
        table,
        lax.all_to_all(returned[None], "sector", split_axis=1, concat_axis=0, tiled=True).astype(
            jnp.float32
        ),
        precision=highest,
    )
    back = lax.all_to_all(
        mixed.astype(jnp.bfloat16), "sector", split_axis=0, concat_axis=1, tiled=True
    )[0]
    stress_field = jnp.dot(back, stress_basis, preferred_element_type=jnp.float32).astype(
        jnp.bfloat16
    )
    return stress_field[None]


def solution(mesh):
    return jax.shard_map(
        local,
        mesh=mesh,
        in_specs=(
            P("sector", None, "dof"),
            P("dof", None),
            P("sector", None, None),
            P(None, "dof"),
            P("sector", None),
            P("sector", None),
            P("sector"),
            P(),
        ),
        out_specs=P("sector", None, "dof"),
        check_vma=False,
    )
```

profile of v0, /device:TPU:1, one launch (start us, length us, event | category | flops | bytes accessed | tf_op | source)
XLA Modules:
  0.0 171.5 jit_solution(9315487925137367451)
XLA Ops:
  6.5 0.0 copy-start
  6.5 0.0 copy-start.3
  6.5 0.0 copy-start.1
  6.5 0.0 all-reduce.2.cloned.1.call-start
  6.5 4.1 %fusion.3 = bf16[1,64,1536]{2,1,0:T(8,128)(2,1)} fusion(bf16[1536,1536]{1,0:T(8,128)(2,1)} %param.9, bf16[1,64,1536]{2,1,0:T(8,128)(2,1)} %param.8), kind=kOutput, calls=%fused_computation.9 | convolution fusion | flops 302088192 | bytes 5111808 | tf_op jit(solution)/shard_map/dot_general | solution.py:50
  10.7 0.0 copy-start.2
  10.7 0.0 all-reduce.2.cloned.1.call-update
  10.7 0.0 copy-done.3
  10.7 48.4 %all-reduce.2.cloned.1.call-done = bf16[1,64,1536]{2,1,0:T(8,128)(2,1)} async-done(((bf16[1,64,1536]{2,1,0:T(8,128)(2,1)}), bf16[1,64,1536]{2,1,0:T(8,128)(2,1)}) %all-reduce.2.cloned.1.call-update) | async-done | bytes 196624 | tf_op jit(solution)/shard_map/psum | solution.py:53
  59.1 1.2 copy.52
  60.3 0.6 broadcast.55
  60.9 1.8 %reduce.2 = bf16[64,1536]{1,0:T(8,128)(2,1)S(1)} reduce(bf16[64,1,1536]{2,1,0:T(2,128)(2,1)S(1)} %bitcast.50, bf16[]{:T(256)} %broadcast.55), dimensions={1}, to_apply=%bitcast.48.reduce_sub_computation | reduce | bytes 393218
  62.8 0.7 reshape.75
  63.5 12.8 %all-to-all-start = ((bf16[64,2,768]{2,1,0:T(2,128)(2,1)}), bf16[64,2,768]{2,1,0:T(2,128)(2,1)S(1)}, u32[]{:S(2)}, u32[]{:S(2)}) async-start(bf16[64,2,768]{2,1,0:T(2,128)(2,1)} %reshape.75), calls=%async_computation | async-start | bytes 393216 | tf_op jit(solution)/shard_map/all_to_all | solution.py:57
  77.0 11.3 %all-to-all-done = bf16[64,2,768]{2,1,0:T(2,128)(2,1)S(1)} async-done(((bf16[64,2,768]{2,1,0:T(2,128)(2,1)}), bf16[64,2,768]{2,1,0:T(2,128)(2,1)S(1)}, u32[]{:S(2)}, u32[]{:S(2)}) %all-to-all-start) | async-done | bytes 196640 | tf_op jit(solution)/shard_map/all_to_all | solution.py:57
  88.3 0.1 reshape.76
  88.5 0.5 fusion
  89.0 0.8 reduce.3
  89.8 0.7 reshape.77
  90.5 4.5 %all-to-all-start.1 = ((bf16[64,2,768]{2,1,0:T(2,128)(2,1)}), bf16[64,2,768]{2,1,0:T(2,128)(2,1)S(1)}, u32[]{:S(2)}, u32[]{:S(2)}) async-start(bf16[64,2,768]{2,1,0:T(2,128)(2,1)} %reshape.77), calls=%async_computation.1 | async-start | bytes 393216 | tf_op jit(solution)/shard_map/all_to_all | solution.py:62
  95.0 0.0 copy-done.1
  95.0 12.1 %all-to-all-done.1 = bf16[64,2,768]{2,1,0:T(2,128)(2,1)S(1)} async-done(((bf16[64,2,768]{2,1,0:T(2,128)(2,1)}), bf16[64,2,768]{2,1,0:T(2,128)(2,1)S(1)}, u32[]{:S(2)}, u32[]{:S(2)}) %all-to-all-start.1) | async-done | bytes 196640 | tf_op jit(solution)/shard_map/all_to_all | solution.py:62
  107.1 0.1 reshape.78
  107.2 0.0 copy-done
  107.2 0.2 fusion.5
  107.5 0.0 copy-done.2
  107.5 16.2 %multiply_reduce_fusion = bf16[256,64]{0,1:T(8,128)(2,1)S(1)} fusion(f32[256,64]{0,1:T(8,128)S(1)} %fusion.5, f32[256]{0:T(256)S(1)} %bitcast.56, f32[64,64]{1,0:T(8,128)S(1)} %maximum_convert_fusion, f32[256]{0:T(256)S(1)} %bitcast.55, f32[256]{0:T(256)S(1)} %bitcast.54, pred[64,64]{1,0:T(8,128)(4,1)S(1)} %fusion.21), kind=kLoop, calls=%fused_computation | loop fusion | flops 7323648 | bytes 121856
  123.8 0.1 copy.27
  123.9 0.4 fusion.1
  124.2 0.3 copy.51
  124.6 1.8 %reduce.4 = bf16[64,1536]{1,0:T(8,128)(2,1)S(1)} reduce(bf16[64,1,1536]{2,1,0:T(2,128)(2,1)S(1)} %bitcast.51, bf16[]{:T(256)} %broadcast.55), dimensions={1}, to_apply=%bitcast.47.reduce_sub_computation | reduce | bytes 393218
  126.4 0.1 reshape.79
  126.5 16.2 %all_to_all.16 = bf16[64,2,768]{2,1,0:T(2,128)(2,1)S(1)} all-to-all(bf16[64,2,768]{2,1,0:T(2,128)(2,1)S(1)} %reshape.79), channel_id=1, replica_groups=mesh['sector'=64,'dof'=4] {'sector'}, dimensions={0} | all-to-all | bytes 393216 | tf_op jit(solution)/shard_map/all_to_all | solution.py:75
  142.7 0.1 reshape.80
  142.8 0.6 fusion.2
  143.4 0.8 reduce.5
  144.2 0.1 reshape.81
  144.3 16.3 %all_to_all.17 = bf16[64,2,768]{2,1,0:T(2,128)(2,1)S(1)} all-to-all(bf16[64,2,768]{2,1,0:T(2,128)(2,1)S(1)} %reshape.81), channel_id=1, replica_groups=mesh['sector'=64,'dof'=4] {'sector'}, dimensions={0} | all-to-all | bytes 393216 | tf_op jit(solution)/shard_map/all_to_all | solution.py:80
  160.6 0.1 reshape.82
  160.7 3.9 %fusion.4 = bf16[1,64,1536]{2,1,0:T(8,128)(2,1)} fusion(bf16[1536,1536]{1,0:T(8,128)(2,1)} %param.11, bf16[64,1,1536]{2,1,0:T(2,128)(2,1)S(1)} %reshape.82), kind=kOutput, calls=%fused_computation.10 | convolution fusion | flops 302088192 | bytes 5111808 | tf_op jit(solution)/shard_map/dot_general | solution.py:83
  (7 shorter events, 0.1 us)
Async XLA Ops:
  6.5 100.7 %copy-start = (bf16[1,1536,256]{2,1,0:T(8,128)(2,1)S(1)}, bf16[1,1536,256]{2,1,0:T(8,128)(2,1)}, u32[]{:S(2)}) copy-start(bf16[1,1536,256]{2,1,0:T(8,128)(2,1)} %param.10) | copy-start | bytes 2359300
  6.5 4.2 %copy-start.3 = (s32[64]{0:T(128)S(1)}, s32[64]{0:T(128)}, u32[]{:S(2)}) copy-start(s32[64]{0:T(128)} %param.15) | copy-start | bytes 772
  6.5 88.4 %copy-start.1 = (f32[1,256]{1,0:T(1,128)S(1)}, f32[1,256]{1,0:T(1,128)}, u32[]{:S(2)}) copy-start(f32[1,256]{1,0:T(1,128)} %param.12) | copy-start | bytes 3076
  6.5 52.5 %all-reduce.2.cloned.1.call-start = ((), (), s32[]{:S(2)}) async-start(), calls=%async_computation.4 | async-start | bytes 393216 | tf_op jit(solution)/shard_map/psum | solution.py:53
  10.7 96.8 %copy-start.2 = (f32[1,256]{1,0:T(1,128)S(1)}, f32[1,256]{1,0:T(1,128)}, u32[]{:S(2)}) copy-start(f32[1,256]{1,0:T(1,128)} %param.13) | copy-start | bytes 3076
  63.5 24.8 %all-to-all-start = ((bf16[64,2,768]{2,1,0:T(2,128)(2,1)}), bf16[64,2,768]{2,1,0:T(2,128)(2,1)S(1)}, u32[]{:S(2)}, u32[]{:S(2)}) async-start(bf16[64,2,768]{2,1,0:T(2,128)(2,1)} %reshape.75), calls=%async_computation | async-start | bytes 393216 | tf_op jit(solution)/shard_map/all_to_all | solution.py:57
  90.5 16.6 %all-to-all-start.1 = ((bf16[64,2,768]{2,1,0:T(2,128)(2,1)}), bf16[64,2,768]{2,1,0:T(2,128)(2,1)S(1)}, u32[]{:S(2)}, u32[]{:S(2)}) async-start(bf16[64,2,768]{2,1,0:T(2,128)(2,1)} %reshape.77), calls=%async_computation.1 | async-start | bytes 393216 | tf_op jit(solution)/shard_map/all_to_all | solution.py:62
Sparse Core Ops, SparseCore 0:
  10.8 48.2 all-reduce.1
where the time goes:
time: 172 us; the launch traced here: 171 us
  waiting for transfers between devices  71.8 us (42%)
  blocking collectives  32.5 us (19%)
  other arithmetic  21.5 us (12%)
  starting transfers between devices  17.3 us (10%)
  between operations  14.2 us (8%)
  matrix products  9.72 us (6%)
  local copies, waits for them, and re-layouts  4.4 us (3%)
    psum x1, waiting for transfers between devices, local(): reduced = lax.psum(partial_value.astype(jnp.bfloat16), 'dof')  48.4 us
    unnamed x3, other arithmetic  19.9 us
    all_to_all x1, blocking collectives, local(): lax.all_to_all(mixed.astype(jnp.bfloat16), 'sector', split_axis=0, concat...  16.3 us
    all_to_all x1, blocking collectives, local(): lax.all_to_all(returned[None], 'sector', split_axis=1, concat_axis=0, til...  16.2 us
    all_to_all x1, starting transfers between devices, local(): lax.all_to_all(reduced[None], 'sector', split_axis=1, concat_axis=0, tile...  12.8 us
    all_to_all x1, waiting for transfers between devices, local(): lax.all_to_all(mixed.astype(jnp.bfloat16), 'sector', split_axis=0, concat...  12.1 us
    all_to_all x1, waiting for transfers between devices, local(): lax.all_to_all(reduced[None], 'sector', split_axis=1, concat_axis=0, tile...  11.3 us
    all_to_all x1, starting transfers between devices, local(): lax.all_to_all(mixed.astype(jnp.bfloat16), 'sector', split_axis=0, concat...  4.47 us
  transfers between devices with their start and end apart: 3, of which 3 were waited for; matrix products, arithmetic and copies ran while one was open for 0% of the time, Pallas kernels for 0%

commit v1 on v0

--- a/solution.py
+++ b/solution.py
@@ -59,8 +59,14 @@
         ),
         precision=highest,
     )
-    spectrum = lax.all_to_all(
-        mixed.astype(jnp.bfloat16), "sector", split_axis=0, concat_axis=1, tiled=True
+    spectrum = jnp.concatenate(
+        lax.all_to_all(
+            jnp.stack(jnp.split(mixed.astype(jnp.bfloat16), lax.axis_size("sector"), axis=0)),
+            "sector",
+            0,
+            0,
+        ),
+        axis=1,
     )[0]
     modal = jnp.dot(spectrum, modes_slot, preferred_element_type=jnp.float32) * live[None, :]
     response = jnp.einsum("mtu,um->tm", kernel, modal, precision=highest)

time: 172 us -> 174 us (1.012)
    another operation x0 -> x1, other arithmetic: none -> 1.83 us  [local(): jnp.stack(jnp.split(mixed.astype(jnp.bfloat16), lax.axis_size('sector'),...]
    unnamed x17 -> x80, local copies, waits for them, and re-layouts: 2.75 us -> 3.81 us
where the time goes in v1:
time: 174 us
  waiting for transfers between devices  71.8 us (41%)
  blocking collectives  32.5 us (19%)
  other arithmetic  22.6 us (13%)
  starting transfers between devices  17.3 us (10%)
  between operations  14.5 us (8%)
  matrix products  9.72 us (6%)
  local copies, waits for them, and re-layouts  5.48 us (3%)
    psum x1, waiting for transfers between devices, local(): reduced = lax.psum(partial_value.astype(jnp.bfloat16), 'dof')  48.4 us
    unnamed x3, other arithmetic  19.9 us
    all_to_all x1, blocking collectives, local(): lax.all_to_all(mixed.astype(jnp.bfloat16), 'sector', split_axis=0, concat...  16.3 us
    all_to_all x1, blocking collectives, local(): lax.all_to_all(returned[None], 'sector', split_axis=1, concat_axis=0, til...  16.2 us
    all_to_all x1, starting transfers between devices, local(): lax.all_to_all(reduced[None], 'sector', split_axis=1, concat_axis=0, tile...  12.8 us
    all_to_all x1, waiting for transfers between devices, local(): lax.all_to_all(jnp.stack(jnp.split(mixed.astype(jnp.bfloat16), lax.axis_s...  12.1 us
    all_to_all x1, waiting for transfers between devices, local(): lax.all_to_all(reduced[None], 'sector', split_axis=1, concat_axis=0, tile...  11.3 us
    all_to_all x1, starting transfers between devices, local(): lax.all_to_all(jnp.stack(jnp.split(mixed.astype(jnp.bfloat16), lax.axis_s...  4.47 us
  transfers between devices with their start and end apart: 3, of which 3 were waited for; matrix products, arithmetic and copies ran while one was open for 0% of the time, Pallas kernels for 0%

profile of v1, /device:TPU:1, one launch (start us, length us, event | category | flops | bytes accessed | tf_op | source)
XLA Modules:
  0.0 173.9 jit_solution(2761058773107352340)
XLA Ops:
  6.5 0.0 copy-start
  6.5 0.0 copy-start.3
  6.5 0.0 copy-start.1
  6.5 0.0 all-reduce.2.cloned.1.call-start
  6.5 4.1 %fusion.2 = bf16[1,64,1536]{2,1,0:T(8,128)(2,1)} fusion(bf16[1536,1536]{1,0:T(8,128)(2,1)} %param.9, bf16[1,64,1536]{2,1,0:T(8,128)(2,1)} %param.8), kind=kOutput, calls=%fused_computation.8 | convolution fusion | flops 302088192 | bytes 5111808 | tf_op jit(solution)/shard_map/dot_general | solution.py:50
  10.7 0.0 copy-start.2
  10.7 0.0 all-reduce.2.cloned.1.call-update
  10.7 0.0 copy-done.3
  10.7 48.4 %all-reduce.2.cloned.1.call-done = bf16[1,64,1536]{2,1,0:T(8,128)(2,1)} async-done(((bf16[1,64,1536]{2,1,0:T(8,128)(2,1)}), bf16[1,64,1536]{2,1,0:T(8,128)(2,1)}) %all-reduce.2.cloned.1.call-update) | async-done | bytes 196624 | tf_op jit(solution)/shard_map/psum | solution.py:53
  59.1 1.2 copy.49
  60.3 0.6 broadcast.55
  60.9 1.8 %reduce.2 = bf16[64,1536]{1,0:T(8,128)(2,1)S(1)} reduce(bf16[64,1,1536]{2,1,0:T(2,128)(2,1)S(1)} %bitcast.304, bf16[]{:T(256)} %broadcast.55), dimensions={1}, to_apply=%bitcast.302.reduce_sub_computation | reduce | bytes 393218
  62.8 0.7 reshape.199
  63.5 12.8 %all-to-all-start = ((bf16[64,2,768]{2,1,0:T(2,128)(2,1)}), bf16[64,2,768]{2,1,0:T(2,128)(2,1)S(1)}, u32[]{:S(2)}, u32[]{:S(2)}) async-start(bf16[64,2,768]{2,1,0:T(2,128)(2,1)} %reshape.199), calls=%async_computation | async-start | bytes 393216 | tf_op jit(solution)/shard_map/all_to_all | solution.py:57
  77.0 11.3 %all-to-all-done = bf16[64,2,768]{2,1,0:T(2,128)(2,1)S(1)} async-done(((bf16[64,2,768]{2,1,0:T(2,128)(2,1)}), bf16[64,2,768]{2,1,0:T(2,128)(2,1)S(1)}, u32[]{:S(2)}, u32[]{:S(2)}) %all-to-all-start) | async-done | bytes 196640 | tf_op jit(solution)/shard_map/all_to_all | solution.py:57
  88.3 0.1 reshape.200
  88.5 0.5 convolution_convert_fusion.3
  90.3 1.8 %reduce.3 = bf16[64,1536]{1,0:T(8,128)(2,1)S(1)} reduce(bf16[64,1,1,1536]{3,2,1,0:T(2,128)(2,1)S(1)} %constant_dynamic-update-slice_fusion, bf16[]{:T(256)} %broadcast.55), dimensions={1,2}, to_apply=%constant_dynamic-update-slice_fusion.reduce_sub_computation | reduce | bytes 393218 | tf_op jit(solution)/shard_map/stack | solution.py:64
  92.2 0.7 reshape.201
  92.9 4.5 %all-to-all-start.1 = ((bf16[64,2,768]{2,1,0:T(2,128)(2,1)}), bf16[64,2,768]{2,1,0:T(2,128)(2,1)S(1)}, u32[]{:S(2)}, u32[]{:S(2)}) async-start(bf16[64,2,768]{2,1,0:T(2,128)(2,1)} %reshape.201), calls=%async_computation.1 | async-start | bytes 393216 | tf_op jit(solution)/shard_map/all_to_all | solution.py:63
  97.4 0.0 copy-done.1
  97.4 12.1 %all-to-all-done.1 = bf16[64,2,768]{2,1,0:T(2,128)(2,1)S(1)} async-done(((bf16[64,2,768]{2,1,0:T(2,128)(2,1)}), bf16[64,2,768]{2,1,0:T(2,128)(2,1)S(1)}, u32[]{:S(2)}, u32[]{:S(2)}) %all-to-all-start.1) | async-done | bytes 196640 | tf_op jit(solution)/shard_map/all_to_all | solution.py:63
  109.5 0.1 reshape.202
  109.7 0.0 copy-done
  109.7 0.2 fusion.4
  109.9 0.0 copy-done.2
  109.9 16.2 %multiply_reduce_fusion = bf16[256,64]{0,1:T(8,128)(2,1)S(1)} fusion(f32[256,64]{0,1:T(8,128)S(1)} %fusion.4, f32[256]{0:T(256)S(1)} %bitcast.310, f32[64,64]{1,0:T(8,128)S(1)} %maximum_convert_fusion, f32[256]{0:T(256)S(1)} %bitcast.309, f32[256]{0:T(256)S(1)} %bitcast.308, pred[64,64]{1,0:T(8,128)(4,1)S(1)} %fusion.20), kind=kLoop, calls=%fused_computation | loop fusion | flops 7323648 | bytes 121856
  126.2 0.1 copy.24
  126.3 0.4 fusion
  126.7 0.3 copy.48
  127.0 1.8 %reduce.4 = bf16[64,1536]{1,0:T(8,128)(2,1)S(1)} reduce(bf16[64,1,1536]{2,1,0:T(2,128)(2,1)S(1)} %bitcast.305, bf16[]{:T(256)} %broadcast.55), dimensions={1}, to_apply=%bitcast.301.reduce_sub_computation | reduce | bytes 393218
  128.8 0.1 reshape.203
  128.9 16.2 %all_to_all.32 = bf16[64,2,768]{2,1,0:T(2,128)(2,1)S(1)} all-to-all(bf16[64,2,768]{2,1,0:T(2,128)(2,1)S(1)} %reshape.203), channel_id=1, replica_groups=mesh['sector'=64,'dof'=4] {'sector'}, dimensions={0} | all-to-all | bytes 393216 | tf_op jit(solution)/shard_map/all_to_all | solution.py:81
  145.1 0.1 reshape.204
  145.3 0.6 fusion.1
  145.8 0.8 reduce.5
  146.6 0.1 reshape.205
  146.7 16.3 %all_to_all.33 = bf16[64,2,768]{2,1,0:T(2,128)(2,1)S(1)} all-to-all(bf16[64,2,768]{2,1,0:T(2,128)(2,1)S(1)} %reshape.205), channel_id=1, replica_groups=mesh['sector'=64,'dof'=4] {'sector'}, dimensions={0} | all-to-all | bytes 393216 | tf_op jit(solution)/shard_map/all_to_all | solution.py:86
  163.0 0.1 reshape.206
  163.1 3.9 %fusion.3 = bf16[1,64,1536]{2,1,0:T(8,128)(2,1)} fusion(bf16[1536,1536]{1,0:T(8,128)(2,1)} %param.11, bf16[64,1,1536]{2,1,0:T(2,128)(2,1)S(1)} %reshape.206), kind=kOutput, calls=%fused_computation.9 | convolution fusion | flops 302088192 | bytes 5111808 | tf_op jit(solution)/shard_map/dot_general | solution.py:89
  (71 shorter events, 1.1 us)
Async XLA Ops:
  6.5 103.1 %copy-start = (bf16[1,1536,256]{2,1,0:T(8,128)(2,1)S(1)}, bf16[1,1536,256]{2,1,0:T(8,128)(2,1)}, u32[]{:S(2)}) copy-start(bf16[1,1536,256]{2,1,0:T(8,128)(2,1)} %param.10) | copy-start | bytes 2359300
  6.5 4.2 %copy-start.3 = (s32[64]{0:T(128)S(1)}, s32[64]{0:T(128)}, u32[]{:S(2)}) copy-start(s32[64]{0:T(128)} %param.15) | copy-start | bytes 772
  6.5 90.9 %copy-start.1 = (f32[1,256]{1,0:T(1,128)S(1)}, f32[1,256]{1,0:T(1,128)}, u32[]{:S(2)}) copy-start(f32[1,256]{1,0:T(1,128)} %param.12) | copy-start | bytes 3076
  6.5 52.5 %all-reduce.2.cloned.1.call-start = ((), (), s32[]{:S(2)}) async-start(), calls=%async_computation.4 | async-start | bytes 393216 | tf_op jit(solution)/shard_map/psum | solution.py:53
  10.7 99.3 %copy-start.2 = (f32[1,256]{1,0:T(1,128)S(1)}, f32[1,256]{1,0:T(1,128)}, u32[]{:S(2)}) copy-start(f32[1,256]{1,0:T(1,128)} %param.13) | copy-start | bytes 3076
  63.5 24.8 %all-to-all-start = ((bf16[64,2,768]{2,1,0:T(2,128)(2,1)}), bf16[64,2,768]{2,1,0:T(2,128)(2,1)S(1)}, u32[]{:S(2)}, u32[]{:S(2)}) async-start(bf16[64,2,768]{2,1,0:T(2,128)(2,1)} %reshape.199), calls=%async_computation | async-start | bytes 393216 | tf_op jit(solution)/shard_map/all_to_all | solution.py:57
  92.9 16.6 %all-to-all-start.1 = ((bf16[64,2,768]{2,1,0:T(2,128)(2,1)}), bf16[64,2,768]{2,1,0:T(2,128)(2,1)S(1)}, u32[]{:S(2)}, u32[]{:S(2)}) async-start(bf16[64,2,768]{2,1,0:T(2,128)(2,1)} %reshape.201), calls=%async_computation.1 | async-start | bytes 393216 | tf_op jit(solution)/shard_map/all_to_all | solution.py:63
Sparse Core Ops, SparseCore 0:
  10.8 48.2 all-reduce.1
